TPU v7x, 128 devices: a whole 4x4x4 slice. The times are simulated.
128 devices in a mesh: rows: 8 (over y, z_lo), pairs: 16 (over z_hi, x, core).
Axes of the slice: x: 4, y: 4, z: 4 (z_hi: 2, z_lo: 2; z = z_hi * 2 + z_lo), core: 2. Of those that a mesh axis runs over, the one named last changes fastest.
Arguments:
- unit_rows: float32 [8, 16, 192, 8192], P('rows', 'pairs'), may hold values from -6 to 6
- unit_counts: int32 [8, 16], P('rows'), may hold values from 1 to 192, 1024 in all within a row
- seating: int32 [32], replicated, may hold values from 0 to 31, each once
- channel_scale: float32 [8192], replicated, may hold values from 0.25 to 4
Outputs:
- rotated: float32 [8192, 8192], P('rows', 'pairs')
Inputs may be any that keep to these rules, and one draw needn't show every extreme that they name: `unit_counts`: each row of 16 counts sums to 1024, and in each row the largest is exactly 192. `seating`: each block once.
All inputs are finite; a program needn't handle non-finite values.
Results may differ from a plain program's by a relative error of at most 0.0001.
Values sent between devices are 32-bit elements; how exact they have to be, the bound alone decides.
No kernel may reach another device: no remote copies, remote signals or barrier semaphores. Data moves between devices by JAX's collectives and lax.ppermute only.
A program may use at most 128 MiB of HBM per device.

v0:
```python
import jax
import jax.numpy as jnp
from jax import lax
from jax.sharding import PartitionSpec as P

ROWS_DEV = 1024
BLOCK = 256
ROUNDS = 2
epsilon = 1e-06
HI = lax.Precision.HIGHEST
NEWTON_TOL_SQ = 0.0001
NEWTON_MAX = 60


def passed_along(array, axis, by):
    length = lax.axis_size(axis)
    pairs = [(i, i + by) for i in range(length) if 0 <= i + by < length]
    return lax.ppermute(array, axis, pairs)


def spd_inverse(sym_part):
    n = sym_part.shape[0]
    identity = jnp.eye(n, dtype=jnp.float32)
    bound = jnp.max(jnp.sum(jnp.abs(sym_part), axis=1))
    scale = 2.0 / (1.0 + bound)
    inverse = scale * identity
    residual = identity - scale * sym_part

    def cond(state):
        step, _, _, err = state
        return jnp.logical_and(err > NEWTON_TOL_SQ, step < NEWTON_MAX)

    def body(state):
        step, inverse, residual, _ = state
        inverse = inverse + jnp.dot(inverse, residual, precision=HI)
        residual = identity - jnp.dot(sym_part, inverse, precision=HI)
        return (step + 1, inverse, residual, jnp.sum(residual * residual))

    state = (jnp.int32(0), inverse, residual, jnp.sum(residual * residual))
    _, inverse, residual, _ = lax.while_loop(cond, body, state)
    inverse = inverse + jnp.dot(inverse, residual, precision=HI)
    residual = identity - jnp.dot(sym_part, inverse, precision=HI)
    inverse = inverse + jnp.dot(inverse, residual, precision=HI)
    return inverse


def rotate(panels):
    partial_gram = lax.dot_general(
        panels, panels, (((0,), (0,)), ((), ())), precision=HI, preferred_element_type=jnp.float32
    )
    gram_full = lax.psum(partial_gram, "rows")
    diag_terms = jnp.diagonal(gram_full)
    skew_part = (
        gram_full
        * (diag_terms[None, :] - diag_terms[:, None])
        / (2.0 * (diag_terms[:, None] ** 2 + diag_terms[None, :] ** 2) + epsilon)
    )
    skew_square = jnp.dot(skew_part, skew_part, precision=HI)
    identity = jnp.eye(skew_part.shape[0], dtype=jnp.float32)
    numerator = identity + skew_part + 0.25 * skew_square
    sym_part = identity - 0.25 * skew_square
    rotation = jnp.dot(numerator, spd_inverse(sym_part), precision=HI)
    return jnp.dot(panels, rotation, precision=HI)


def advance(panels):
    half_width = panels.shape[1] // 2
    upper = panels[:, :half_width]
    lower = panels[:, half_width:]
    pair_index = lax.axis_index("pairs")
    last_pair = lax.axis_size("pairs") - 1
    upward = jnp.where(pair_index == 0, lower, upper)
    came_up = passed_along(upward, "pairs", 1)
    came_down = passed_along(lower, "pairs", -1)
    new_upper = jnp.where(pair_index == 0, upper, came_up)
    new_lower = jnp.where(pair_index == last_pair, upper, came_down)
    return jnp.concatenate([new_upper, new_lower], axis=1)


def compact(panels, group_counts, capacity):
    unit_ends = jnp.cumsum(group_counts)
    target = lax.iota(jnp.int32, ROWS_DEV)
    passed = (target[:, None] >= unit_ends[None, :]).astype(jnp.int32)
    owner_unit = jnp.sum(passed, axis=1)
    owner_start = jnp.sum(passed * group_counts[None, :], axis=1)
    source = owner_unit * capacity + target - owner_start
    return jnp.take(panels, source, axis=0)


def local(unit_rows, unit_counts, seating, channel_scale):
    capacity = unit_rows.shape[2]
    columns = unit_rows.shape[3]
    group_counts = unit_counts[0]
    scaled = unit_rows[0, 0] * channel_scale[None, :]
    seated = jnp.take(scaled.reshape(capacity, columns // BLOCK, BLOCK), seating, axis=1).reshape(
        capacity, columns
    )
    panels = lax.all_to_all(seated, "pairs", split_axis=1, concat_axis=0, tiled=True)
    current = compact(panels, group_counts, capacity)
    for round_index in range(ROUNDS):
        current = rotate(current)
        if round_index + 1 < ROUNDS:
            current = advance(current)
    return current


def solution(mesh):
    return jax.shard_map(
        local,
        mesh=mesh,
        in_specs=(P("rows", "pairs", None, None), P("rows", None), P(), P()),
        out_specs=P("rows", "pairs"),
        check_vma=False,
    )
```

profile of v0, /device:TPU:2, one launch (start us, length us, event | category | flops | bytes accessed | tf_op | source)
XLA Modules:
  0.0 489.8 jit_solution(11899552848003923042)
XLA Ops:
  7.9 7.8 %copy.44 = f32[24,8,32,256]{3,2,1,0:T(8,128)} copy(f32[24,8,32,256]{3,1,2,0:T(8,128)} %bitcast.66) | data formatting | bytes 12582912
  15.7 9.1 %copy_multiply_fusion = f32[192,32,256]{2,0,1:T(8,128)} fusion(f32[192,32,256]{2,1,0:T(8,128)} %bitcast.64, f32[32,256]{1,0:T(8,128)S(1)} %mul.96), kind=kLoop, calls=%fused_computation.16 | loop fusion | flops 1572864 | bytes 12615680 | tf_op jit(solution)/shard_map/mul | solution.py:94
  24.8 6.4 %gather_fusion = f32[32,192,256]{2,1,0:T(8,128)} fusion(f32[192,32,256]{2,0,1:T(8,128)} %copy_multiply_fusion, s32[1024]{0:T(1024)S(1)} %pad_clamp_fusion), kind=kCustom, calls=%fused_computation | custom fusion | bytes 12583040 | tf_op jit(solution)/shard_map/jit(_take)/gather | solution.py:95
  31.2 9.1 %copy.35 = f32[192,32,256]{2,1,0:T(8,128)} copy(f32[192,32,256]{2,0,1:T(8,128)} %bitcast.65) | data formatting | bytes 12582912 | tf_op jit(solution)/shard_map/jit(_take)/gather | solution.py:95
  40.3 7.7 %gather.18 = f32[192,16,512]{2,1,0:T(8,128)} reshape(f32[192,32,256]{2,1,0:T(8,128)} %copy.35) | data formatting | bytes 12582912 | tf_op jit(solution)/shard_map/jit(_take)/gather | solution.py:95
  51.8 6.3 %copy.36 = f32[192,16,512]{2,0,1:T(8,128)} copy(f32[192,16,512]{2,1,0:T(8,128)S(1)} %broadcast_select_fusion) | data formatting | bytes 12582912 | tf_op jit(solution)/shard_map/jit(_take)/select_n | solution.py:95
  58.1 8.3 %all-to-all-start = ((f32[192,16,512]{2,0,1:T(8,128)}), f32[192,16,512]{2,0,1:T(8,128)}, u32[]{:S(2)}, u32[]{:S(2)}) async-start(f32[192,16,512]{2,0,1:T(8,128)} %copy.36), calls=%async_computation | async-start | bytes 12582912 | tf_op jit(solution)/shard_map/all_to_all | solution.py:98
  66.8 84.9 %all-to-all-done = f32[192,16,512]{2,0,1:T(8,128)} async-done(((f32[192,16,512]{2,0,1:T(8,128)}), f32[192,16,512]{2,0,1:T(8,128)}, u32[]{:S(2)}, u32[]{:S(2)}) %all-to-all-start) | async-done | bytes 6291488 | tf_op jit(solution)/shard_map/all_to_all | solution.py:98
  151.7 6.8 %gather_fusion.1 = f32[1024,512]{1,0:T(8,128)S(1)} fusion(f32[3072,512]{1,0:T(8,128)} %bitcast.4, s32[1024]{0:T(1024)S(1)} %broadcast_clamp_fusion), kind=kCustom, calls=%fused_computation.1 | custom fusion | bytes 4198400 | tf_op jit(solution)/shard_map/jit(_take)/gather | solution.py:87
  158.6 5.2 %fusion.8 = f32[512,512]{1,0:T(8,128)} fusion(f32[1024,512]{1,0:T(8,128)S(1)} %gather_fusion.1, pred[1024]{0:T(1024)(128)(4,1)S(1)} %compare_and_fusion), kind=kOutput, calls=%fused_computation.29 | convolution fusion | flops 3221749760 | bytes 3146752 | tf_op jit(solution)/shard_map/dot_general | solution.py:48
  163.9 77.8 %all-reduce.3.cloned.1.call-done = f32[512,512]{1,0:T(8,128)} async-done(((f32[512,512]{1,0:T(8,128)}), f32[512,512]{1,0:T(8,128)}) %all-reduce.3.cloned.1.call-update) | async-done | bytes 1048592 | tf_op jit(solution)/shard_map/psum | solution.py:51
  241.7 8.8 %gather_fusion.2 = f32[512]{0:T(512)S(1)} fusion(f32[512,512]{1,0:T(8,128)} %all-reduce.3.cloned.1.call-done, s32[512]{0:T(512)S(1)} %bitcast.62), kind=kCustom, calls=%fused_computation.2 | custom fusion | bytes 8192 | tf_op jit(solution)/shard_map/jit(diagonal)/cond/branch_0_fun/gather | solution.py:52
  257.9 34.8 %while.30 = (s32[]{:T(128)}, f32[512,512]{1,0:T(8,128)S(1)}, f32[512,512]{0,1:T(8,128)S(1)}, f32[]{:T(128)}, f32[512,512]{1,0:T(8,128)S(1)}, /*index=5*/s32[]{:T(128)}) while((s32[]{:T(128)}, f32[512,512]{1,0:T(8,128)S(1)}, f32[512,512]{0,1:T(8,128)S(1)}, f32[]{:T(128)}, f32[512,512]{1,0:T(8,128)S(1)}, /*index=5*/s32[]{:T(128)}) %tuple.63), condition=%wide.region_9.10_spmd.clone, body=%wide.region_7.9_spmd.clone.sunk | while | flops 3222798336 | bytes 8388693 | solution.py:40
  260.5 4.2 multiply_reduce_fusion.6
  267.3 4.2 multiply_reduce_fusion.6
  274.1 4.2 multiply_reduce_fusion.6
  280.9 4.2 multiply_reduce_fusion.6
  287.7 4.2 multiply_reduce_fusion.6
  300.6 3.9 fusion.6
  307.6 3.9 collective-permute-start.1
  311.4 10.6 %collective-permute-done = f32[1024,256]{0,1:T(8,128)} collective-permute-done((f32[1024,256]{0,1:T(8,128)}, f32[1024,256]{0,1:T(8,128)}, u32[]{:S(2)}, u32[]{:S(2)}) %collective-permute-start) | collective-permute-done | bytes 1048608 | tf_op jit(solution)/shard_map/ppermute | solution.py:18
  326.8 4.5 fusion.11
  331.3 81.5 %all-reduce.5.cloned.1.call-done = f32[512,512]{1,0:T(8,128)} async-done(((f32[512,512]{1,0:T(8,128)}), f32[512,512]{1,0:T(8,128)}) %all-reduce.5.cloned.1.call-update) | async-done | bytes 1048592 | tf_op jit(solution)/shard_map/psum | solution.py:51
  412.8 8.6 %gather_fusion.3 = f32[512]{0:T(512)S(1)} fusion(f32[512,512]{1,0:T(8,128)} %all-reduce.5.cloned.1.call-done, s32[512]{0:T(512)S(1)} %bitcast.63), kind=kCustom, calls=%fused_computation.3 | custom fusion | bytes 8192 | tf_op jit(solution)/shard_map/jit(diagonal)/cond/branch_0_fun/gather | solution.py:52
  428.8 41.0 %while.31 = (s32[]{:T(128)}, f32[512,512]{1,0:T(8,128)S(1)}, f32[512,512]{0,1:T(8,128)S(1)}, f32[]{:T(128)}, f32[512,512]{1,0:T(8,128)S(1)}, /*index=5*/s32[]{:T(128)}) while((s32[]{:T(128)}, f32[512,512]{1,0:T(8,128)S(1)}, f32[512,512]{0,1:T(8,128)S(1)}, f32[]{:T(128)}, f32[512,512]{1,0:T(8,128)S(1)}, ...), condition=%wide.region_16.17_spmd.clone, body=%wide.region_14.16_spmd.clone.sunk | while | flops 3222798336 | bytes 8388693 | solution.py:40
  431.4 4.1 multiply_reduce_fusion.7
  438.1 4.1 multiply_reduce_fusion.7
  444.8 4.1 multiply_reduce_fusion.7
  451.5 4.1 multiply_reduce_fusion.7
  458.2 4.1 multiply_reduce_fusion.7
  464.8 4.1 multiply_reduce_fusion.7
  477.7 4.8 fusion.10
  (98 shorter events, 63.6 us)
Async XLA Ops:
  7.9 7.8 %copy-start.14 = (f32[8192]{0:T(1024)S(1)}, f32[8192]{0:T(1024)}, u32[]{:S(2)}) copy-start(f32[8192]{0:T(1024)} %param.11) | copy-start | bytes 98308
  58.0 8.3 %copy-start.15 = (s32[1,16]{1,0:T(1,128)S(1)}, s32[1,16]{1,0:T(1,128)}, u32[]{:S(2)}) copy-start(s32[1,16]{1,0:T(1,128)} %param.9) | copy-start | bytes 196
  58.1 93.7 %all-to-all-start = ((f32[192,16,512]{2,0,1:T(8,128)}), f32[192,16,512]{2,0,1:T(8,128)}, u32[]{:S(2)}, u32[]{:S(2)}) async-start(f32[192,16,512]{2,0,1:T(8,128)} %copy.36), calls=%async_computation | async-start | bytes 12582912 | tf_op jit(solution)/shard_map/all_to_all | solution.py:98
  66.3 175.3 %all-reduce.3.cloned.1.call-start = ((), (), s32[]{:S(2)}) async-start(), calls=%async_computation.1 | async-start | bytes 2097152 | tf_op jit(solution)/shard_map/psum | solution.py:51
  158.5 5.2 %copy-start = (f32[1024,512]{1,0:T(8,128)}, f32[1024,512]{1,0:T(8,128)S(1)}, u32[]{:S(2)}) copy-start(f32[1024,512]{1,0:T(8,128)S(1)} %gather_fusion.1) | copy-start | bytes 6291460
  163.8 249.0 %all-reduce.5.cloned.1.call-start = ((), (), s32[]{:S(2)}) async-start(), calls=%async_computation.2 | async-start | bytes 2097152 | tf_op jit(solution)/shard_map/psum | solution.py:51
  241.7 8.8 %copy-start.10 = (f32[512,512]{1,0:T(8,128)S(1)}, f32[512,512]{1,0:T(8,128)}, u32[]{:S(2)}) copy-start(f32[512,512]{1,0:T(8,128)} %all-reduce.3.cloned.1.call-done) | copy-start | bytes 3145732
  253.0 3.3 copy-start.2
  292.7 1.9 copy-start.3
  296.5 1.9 copy-start.11
  298.4 2.2 copy-start.1
  305.7 16.4 %collective-permute-start = (f32[1024,256]{0,1:T(8,128)}, f32[1024,256]{0,1:T(8,128)}, u32[]{:S(2)}, u32[]{:S(2)}) collective-permute-start(f32[1024,256]{0,1:T(8,128)} %get-tuple-element.181), channel_id=1, source_target_pairs={{0,1},{1,2},{2,3},{3,4},{4,5},{5,6},{6,7},{7,8},{8,9},{9,10},{10,1... | collective-permute-start | bytes 3145736 | tf_op jit(solution)/shard_map/ppermute | solution.py:18
  307.6 15.9 %collective-permute-start.1 = (f32[1024,256]{0,1:T(8,128)S(1)}, f32[1024,256]{0,1:T(8,128)}, u32[]{:S(2)}, u32[]{:S(2)}) collective-permute-start(f32[1024,256]{0,1:T(8,128)S(1)} %get-tuple-element.182), channel_id=1, source_target_pairs={{1,0},{2,1},{3,2},{4,3},{5,4},{6,5},{7,6},{8,7},{9,8},{10,9},{11,1... | collective-permute-start | bytes 3145736 | tf_op jit(solution)/shard_map/ppermute | solution.py:18
  325.4 1.0 copy-start.6
  325.4 1.4 copy-start.8
  412.8 8.6 %copy-start.12 = (f32[512,512]{1,0:T(8,128)S(1)}, f32[512,512]{1,0:T(8,128)}, u32[]{:S(2)}) copy-start(f32[512,512]{1,0:T(8,128)} %all-reduce.5.cloned.1.call-done) | copy-start | bytes 3145732
  423.9 3.3 copy-start.4
  469.8 1.9 copy-start.5
  473.6 1.9 copy-start.13
  475.5 2.2 copy-start.7
  475.5 2.2 copy-start.9
Sparse Core Ops, SparseCore 0:
  163.9 77.7 all-reduce.2
  331.4 81.3 all-reduce.4
where the time goes:
time: 499 us; the launch traced here: 490 us
  waiting for transfers between devices  256 us (51%)
  matrix products  105 us (21%)
  local copies, waits for them, and re-layouts  67 us (13%)
  other arithmetic  22.6 us (5%)
  between operations  15.6 us (3%)
  starting transfers between devices  14.1 us (3%)
  loops' own time  8.89 us (2%)
    psum x2, waiting for transfers between devices, rotate(): gram_full = lax.psum(partial_gram, 'rows')  159 us
    all_to_all x1, waiting for transfers between devices, local(): lax.all_to_all(seated, 'pairs', split_axis=1, concat_axis=0, tiled=True)  84.9 us
    dot_general x11, matrix products, body(): residual = identity - jnp.dot(sym_part, inverse, precision=HI)  45.7 us
    gather x3, local copies, waits for them, and re-layouts, local(): jnp.take(scaled.reshape(capacity, columns // BLOCK, BLOCK), seating, axis=1)  23.2 us
    dot_general x11, matrix products, body(): inverse = inverse + jnp.dot(inverse, residual, precision=HI)  20.5 us
    gather x2, local copies, waits for them, and re-layouts, rotate(): diag_terms = jnp.diagonal(gram_full)  17.4 us
    unnamed x36, local copies, waits for them, and re-layouts  12.3 us
    ppermute x2, waiting for transfers between devices, passed_along(): return lax.ppermute(array, axis, pairs)  12.1 us
  transfers between devices with their start and end apart: 5, of which 5 were waited for; matrix products, arithmetic and copies ran while one was open for 0% of the time, Pallas kernels for 0%

commit v1 on v0

--- a/solution.py
+++ b/solution.py
@@ -2,6 +2,7 @@
 import jax.numpy as jnp
 from jax import lax
 from jax.sharding import PartitionSpec as P
+from jax.lax import all_gather
 
 ROWS_DEV = 1024
 BLOCK = 256
@@ -10,6 +11,11 @@
 HI = lax.Precision.HIGHEST
 NEWTON_TOL_SQ = 0.0001
 NEWTON_MAX = 60
+
+
+def _divide_vectors(xx):
+    r_now = jnp.sum(all_gather(xx, "rows"), axis=0)
+    return r_now
 
 
 def passed_along(array, axis, by):
@@ -48,7 +54,7 @@
     partial_gram = lax.dot_general(
         panels, panels, (((0,), (0,)), ((), ())), precision=HI, preferred_element_type=jnp.float32
     )
-    gram_full = lax.psum(partial_gram, "rows")
+    gram_full = _divide_vectors(partial_gram)
     diag_terms = jnp.diagonal(gram_full)
     skew_part = (
         gram_full

time: 499 us -> 695 us (1.39)
  waiting for transfers between devices: 256 us -> 443 us
  other arithmetic: 22.6 us -> 30 us
    all_gather x0 -> x2, waiting for transfers between devices: none -> 346 us  [_divide_vectors(): r_now = jnp.sum(all_gather(xx, 'rows'), axis=0)]
    psum x2 -> x0, waiting for transfers between devices: 159 us -> none  [rotate(): gram_full = lax.psum(partial_gram, 'rows')]
    reduce_sum x0 -> x2, other arithmetic: none -> 9.06 us  [_divide_vectors(): r_now = jnp.sum(all_gather(xx, 'rows'), axis=0)]
    gather x2, local copies, waits for them, and re-layouts: 17.4 us -> 9.22 us  [rotate(): diag_terms = jnp.diagonal(gram_full)]
where the time goes in v1:
time: 695 us; the launch traced here: 682 us
  waiting for transfers between devices  443 us (64%)
  matrix products  109 us (16%)
  local copies, waits for them, and re-layouts  61.5 us (9%)
  other arithmetic  30 us (4%)
  between operations  15.7 us (2%)
  starting transfers between devices  13.9 us (2%)
  loops' own time  8.69 us (1%)
    all_gather x2, waiting for transfers between devices, _divide_vectors(): r_now = jnp.sum(all_gather(xx, 'rows'), axis=0)  346 us
    all_to_all x1, waiting for transfers between devices, local(): lax.all_to_all(seated, 'pairs', split_axis=1, concat_axis=0, tiled=True)  84.9 us
    dot_general x11, matrix products, body(): residual = identity - jnp.dot(sym_part, inverse, precision=HI)  45.7 us
    gather x3, local copies, waits for them, and re-layouts, local(): jnp.take(scaled.reshape(capacity, columns // BLOCK, BLOCK), seating, axis=1)  23.4 us
    dot_general x11, matrix products, body(): inverse = inverse + jnp.dot(inverse, residual, precision=HI)  20.5 us
  transfers between devices with their start and end apart: 5, of which 5 were waited for; matrix products, arithmetic and copies ran while one was open for 0% of the time, Pallas kernels for 0%

profile of v1, /device:TPU:2, one launch (start us, length us, event | category | flops | bytes accessed | tf_op | source)
XLA Modules:
  0.0 682.3 jit_solution(16112733065544833070)
XLA Ops:
  7.9 7.8 %copy.68 = f32[24,8,32,256]{3,2,1,0:T(8,128)} copy(f32[24,8,32,256]{3,1,2,0:T(8,128)} %bitcast.70) | data formatting | bytes 12582912
  15.7 9.1 %copy_multiply_fusion = f32[192,32,256]{2,0,1:T(8,128)} fusion(f32[192,32,256]{2,1,0:T(8,128)} %bitcast.66, f32[32,256]{1,0:T(8,128)S(1)} %mul.96), kind=kLoop, calls=%fused_computation.16 | loop fusion | flops 1572864 | bytes 12615680 | tf_op jit(solution)/shard_map/mul | solution.py:100
  24.8 6.4 gather_fusion
  31.2 9.1 %copy.55 = f32[192,32,256]{2,1,0:T(8,128)} copy(f32[192,32,256]{2,0,1:T(8,128)} %bitcast.67) | data formatting | bytes 12582912 | tf_op jit(solution)/shard_map/jit(_take)/gather | solution.py:101
  40.3 7.9 %gather.18 = f32[192,16,512]{2,1,0:T(8,128)} reshape(f32[192,32,256]{2,1,0:T(8,128)} %copy.55) | data formatting | bytes 12582912 | tf_op jit(solution)/shard_map/jit(_take)/gather | solution.py:101
  52.0 6.3 copy.56
  58.3 8.3 %all-to-all-start = ((f32[192,16,512]{2,0,1:T(8,128)}), f32[192,16,512]{2,0,1:T(8,128)}, u32[]{:S(2)}, u32[]{:S(2)}) async-start(f32[192,16,512]{2,0,1:T(8,128)} %copy.56), calls=%async_computation | async-start | bytes 12582912 | tf_op jit(solution)/shard_map/all_to_all | solution.py:104
  67.1 84.9 %all-to-all-done = f32[192,16,512]{2,0,1:T(8,128)} async-done(((f32[192,16,512]{2,0,1:T(8,128)}), f32[192,16,512]{2,0,1:T(8,128)}, u32[]{:S(2)}, u32[]{:S(2)}) %all-to-all-start) | async-done | bytes 6291488 | tf_op jit(solution)/shard_map/all_to_all | solution.py:104
  152.0 6.8 gather_fusion.1
  158.8 5.2 fusion.8
  164.2 168.2 %all-gather.5.cloned.1.call-done = f32[4096,512]{1,0:T(8,128)} async-done(((f32[512,512]{1,0:T(8,128)}), f32[4096,512]{1,0:T(8,128)}) %all-gather.5.cloned.1.call-update) | async-done | bytes 8388624 | tf_op jit(solution)/shard_map/all_gather | solution.py:17
  332.4 4.5 reduce_sum.95
  337.2 4.7 gather_fusion.2
  349.9 35.4 %while.30 = (s32[]{:T(128)}, f32[512,512]{1,0:T(8,128)S(1)}, f32[512,512]{0,1:T(8,128)S(1)}, f32[]{:T(128)}, f32[512,512]{1,0:T(8,128)S(1)}, /*index=5*/s32[]{:T(128)}) while((s32[]{:T(128)}, f32[512,512]{1,0:T(8,128)S(1)}, f32[512,512]{0,1:T(8,128)S(1)}, f32[]{:T(128)}, f32[512,512]{1,0:T(8,128)S(1)}, /*index=5*/s32[]{:T(128)}) %tuple.65), condition=%wide.region_9.10_spmd.clone, body=%wide.region_7.9_spmd.clone.sunk | while | flops 3222798336 | bytes 8388693 | solution.py:46
  352.5 4.3 multiply_reduce_fusion.6
  359.3 4.3 multiply_reduce_fusion.6
  366.2 4.3 multiply_reduce_fusion.6
  373.1 4.3 multiply_reduce_fusion.6
  379.9 4.3 multiply_reduce_fusion.6
  404.2 10.8 %collective-permute-done = f32[1024,256]{0,1:T(8,128)} collective-permute-done((f32[1024,256]{0,1:T(8,128)}, f32[1024,256]{0,1:T(8,128)}, u32[]{:S(2)}, u32[]{:S(2)}) %collective-permute-start) | collective-permute-done | bytes 1048608 | tf_op jit(solution)/shard_map/ppermute | solution.py:24
  419.8 4.5 fusion.11
  424.3 177.8 %all-gather.7.cloned.1.call-done = f32[4096,512]{1,0:T(8,128)} async-done(((f32[512,512]{1,0:T(8,128)}), f32[4096,512]{1,0:T(8,128)}) %all-gather.7.cloned.1.call-update) | async-done | bytes 8388624 | tf_op jit(solution)/shard_map/all_gather | solution.py:17
  602.1 4.5 reduce_sum.98
  607.9 4.5 gather_fusion.3
  612.5 5.0 convert_subtract_fusion.1
  621.9 40.3 %while.31 = (s32[]{:T(128)}, f32[512,512]{1,0:T(8,128)S(1)}, f32[512,512]{0,1:T(8,128)S(1)}, f32[]{:T(128)}, f32[512,512]{1,0:T(8,128)S(1)}, /*index=5*/s32[]{:T(128)}) while((s32[]{:T(128)}, f32[512,512]{1,0:T(8,128)S(1)}, f32[512,512]{0,1:T(8,128)S(1)}, f32[]{:T(128)}, f32[512,512]{1,0:T(8,128)S(1)}, ...), condition=%wide.region_16.17_spmd.clone, body=%wide.region_14.16_spmd.clone.sunk | while | flops 3222798336 | bytes 8388693 | solution.py:46
  631.0 4.1 multiply_reduce_fusion.7
  637.6 4.1 multiply_reduce_fusion.7
  644.2 4.1 multiply_reduce_fusion.7
  650.8 4.1 multiply_reduce_fusion.7
  657.4 4.1 multiply_reduce_fusion.7
  670.3 4.8 fusion.10
  (102 shorter events, 74.9 us)
Async XLA Ops:
  7.9 7.8 %copy-start.13 = (f32[8192]{0:T(1024)S(1)}, f32[8192]{0:T(1024)}, u32[]{:S(2)}) copy-start(f32[8192]{0:T(1024)} %param.11) | copy-start | bytes 98308
  58.3 8.3 %copy-start.14 = (s32[1,16]{1,0:T(1,128)S(1)}, s32[1,16]{1,0:T(1,128)}, u32[]{:S(2)}) copy-start(s32[1,16]{1,0:T(1,128)} %param.9) | copy-start | bytes 196
  58.3 93.7 %all-to-all-start = ((f32[192,16,512]{2,0,1:T(8,128)}), f32[192,16,512]{2,0,1:T(8,128)}, u32[]{:S(2)}, u32[]{:S(2)}) async-start(f32[192,16,512]{2,0,1:T(8,128)} %copy.56), calls=%async_computation | async-start | bytes 12582912 | tf_op jit(solution)/shard_map/all_to_all | solution.py:104
  66.6 265.8 %all-gather.5.cloned.1.call-start = ((), (), s32[]{:S(2)}) async-start(), calls=%async_computation.1 | async-start | bytes 9437184 | tf_op jit(solution)/shard_map/all_gather | solution.py:17
  158.8 5.3 copy-start
  164.1 438.0 %all-gather.7.cloned.1.call-start = ((), (), s32[]{:S(2)}) async-start(), calls=%async_computation.2 | async-start | bytes 9437184 | tf_op jit(solution)/shard_map/all_gather | solution.py:17
  337.2 8.2 %copy-start.11 = (f32[512,512]{0,1:T(8,128)}, f32[512,512]{0,1:T(8,128)S(1)}, u32[]{:S(2)}) copy-start(f32[512,512]{0,1:T(8,128)S(1)} %copy.57) | copy-start | bytes 3145732
  345.4 2.6 copy-start.2
  385.3 1.9 copy-start.3
  389.1 1.9 copy-start.12
  391.1 2.3 copy-start.1
  398.6 16.4 %collective-permute-start = (f32[1024,256]{0,1:T(8,128)}, f32[1024,256]{0,1:T(8,128)}, u32[]{:S(2)}, u32[]{:S(2)}) collective-permute-start(f32[1024,256]{0,1:T(8,128)} %get-tuple-element.191), channel_id=1, source_target_pairs={{0,1},{1,2},{2,3},{3,4},{4,5},{5,6},{6,7},{7,8},{8,9},{9,10},{10,1... | collective-permute-start | bytes 3145736 | tf_op jit(solution)/shard_map/ppermute | solution.py:24
  400.6 15.9 %collective-permute-start.1 = (f32[1024,256]{0,1:T(8,128)S(1)}, f32[1024,256]{0,1:T(8,128)}, u32[]{:S(2)}, u32[]{:S(2)}) collective-permute-start(f32[1024,256]{0,1:T(8,128)S(1)} %get-tuple-element.192), channel_id=1, source_target_pairs={{1,0},{2,1},{3,2},{4,3},{5,4},{6,5},{7,6},{8,7},{9,8},{10,9},{11,1... | collective-permute-start | bytes 3145736 | tf_op jit(solution)/shard_map/ppermute | solution.py:24
  418.4 1.0 copy-start.6
  418.4 1.4 copy-start.8
  617.5 2.8 copy-start.4
  662.2 1.9 copy-start.5
  666.0 1.9 copy-start.10
  668.0 2.3 copy-start.7
  668.0 2.3 copy-start.9
Sparse Core Ops, SparseCore 0:
  164.2 168.1 all-gather.4
  424.4 177.6 all-gather.6
